TPU v7x, 32 devices: a whole 2x2x4 slice. The times are simulated.
32 devices in a mesh: row: 4 (over y, x), col: 8 (over z, core).
Axes of the slice: x: 2, y: 2, z: 4, core: 2. Of those that a mesh axis runs over, the one named last changes fastest.
Arguments:
- density: float32 [2048, 2048], P('row', 'col'), as said below
- pattern: int32 [16, 16], replicated, may hold values from 0 to 1, as said below
Outputs:
- purified: float32 [2048, 2048], P('row', 'col')
Inputs may be any that keep to these rules, and one draw needn't show every extreme that they name: density is symmetric and zero outside the blocks that pattern allows. pattern is symmetric with ones on its diagonal, and every block row holds exactly 7 ones.
All inputs are finite; a program needn't handle non-finite values.
Results may differ from a plain program's by a relative error of at most 0.0061.
Values may be sent and summed in bfloat16 or wider, within the bound.
No kernel may reach another device: no remote copies, remote signals or barrier semaphores. Data moves between devices by JAX's collectives and lax.ppermute only.
A program may use at most 64 MiB of HBM per device.

v0:
```python
import jax
import jax.numpy as jnp
from jax import lax
from jax.sharding import PartitionSpec as P

BS = 128
STEPS = 2


def allowed_blocks(pattern):
    count = pattern.shape[0]
    index = lax.iota(jnp.int32, count)
    eye = (index[:, None] == index[None, :]).astype(jnp.int32)
    return jnp.maximum(jnp.maximum(pattern, pattern.T), eye)


def apply_mask(values, blocks):
    row_blocks, col_blocks = blocks.shape
    shaped = values.reshape(row_blocks, BS, col_blocks, BS) * blocks[:, None, :, None]
    return shaped.reshape(row_blocks * BS, col_blocks * BS)


def on_device(density, pattern):
    rows, cols = density.shape
    row_blocks = rows // BS
    col_blocks = cols // BS
    allowed = allowed_blocks(pattern)
    first_row = lax.axis_index("row") * row_blocks
    first_col = lax.axis_index("col") * col_blocks
    blocks = lax.dynamic_slice(allowed, (first_row, first_col), (row_blocks, col_blocks)).astype(
        jnp.float32
    )
    current = apply_mask(density, blocks)
    for step in range(STEPS):
        xb = current.astype(jnp.bfloat16)
        x_panel = lax.all_gather(xb, "row", axis=0, tiled=True)
        square = jnp.dot(
            lax.all_gather(xb, "col", axis=1, tiled=True),
            x_panel,
            preferred_element_type=jnp.float32,
        )
        square = apply_mask(square, blocks)
        qb = square.astype(jnp.bfloat16)
        q_panel = lax.all_gather(qb, "row", axis=0, tiled=True)
        total = jnp.dot(
            lax.all_gather(qb, "col", axis=1, tiled=True),
            x_panel,
            preferred_element_type=jnp.float32,
        )
        jordan = total + jnp.dot(
            lax.all_gather(xb, "col", axis=1, tiled=True),
            q_panel,
            preferred_element_type=jnp.float32,
        )
        current = apply_mask(3.0 * square - jordan, blocks)
    return current


def solution(mesh):
    placed = (P("row", "col"), P())
    return jax.shard_map(
        on_device, mesh=mesh, in_specs=placed, out_specs=P("row", "col"), check_vma=False
    )
```

profile of v0, /device:TPU:0, one launch (start us, length us, event | category | flops | bytes accessed | tf_op | source)
XLA Modules:
  0.0 265.3 jit_solution(4661226299853887989)
XLA Ops:
  6.5 0.0 all-gather.11.cloned.1.call-start
  6.5 0.8 copy.3
  7.3 0.8 fusion.7
  8.1 0.2 mul.53
  8.3 1.8 fusion.5
  10.1 0.0 all-gather.11.cloned.1.call-update
  10.1 0.0 all-gather.9.cloned.1.call-start
  10.2 0.7 all-gather.9.cloned.1.call-update
  10.9 0.0 all-gather.13.cloned.1.call-start
  10.9 28.7 %all-gather.11.cloned.1.call-done = bf16[2048,256]{1,0:T(8,128)(2,1)} async-done(((bf16[512,256]{1,0:T(8,128)(2,1)}), bf16[2048,256]{1,0:T(8,128)(2,1)}) %all-gather.11.cloned.1.call-update) | async-done | bytes 1048592 | tf_op jit(solution)/shard_map/all_gather | solution.py:36
  39.6 32.5 %all-gather.9.cloned.1.call-done = bf16[512,2048]{1,0:T(8,128)(2,1)} async-done(((bf16[512,256]{1,0:T(8,128)(2,1)}), bf16[512,2048]{1,0:T(8,128)(2,1)}) %all-gather.9.cloned.1.call-update) | async-done | bytes 2097168 | tf_op jit(solution)/shard_map/all_gather | solution.py:38
  72.0 3.3 %fusion.8 = (bf16[512,256]{1,0:T(8,128)(2,1)}, f32[512,256]{1,0:T(8,128)S(1)}) fusion(f32[64,8,2,128]{3,2,1,0:T(2,128)S(1)} %bitcast.24, bf16[512,2048]{1,0:T(8,128)(2,1)} %all-gather.9.cloned.1.call-done, bf16[2048,256]{1,0:T(8,128)(2,1)} %all-gather.11.cloned.1.call-done), kind=kOutput, calls=%fused_computation.15 | convolution fusion | flops 537133056 | bytes 4456448 | tf_op jit(solution)/shard_map/dot_general | solution.py:37
  75.3 0.0 all-gather.13.cloned.1.call-update
  75.3 0.0 copy-start.1
  75.3 0.0 all-gather.15.cloned.1.call-start
  75.4 0.5 all-gather.15.cloned.1.call-update
  75.9 0.0 all-gather.19.cloned.1.call-start
  76.0 29.4 %all-gather.13.cloned.1.call-done = bf16[512,2048]{1,0:T(8,128)(2,1)} async-done(((bf16[512,256]{1,0:T(8,128)(2,1)}), bf16[512,2048]{1,0:T(8,128)(2,1)}) %all-gather.13.cloned.1.call-update) | async-done | bytes 2097168 | tf_op jit(solution)/shard_map/all_gather | solution.py:46
  105.4 3.4 %fusion.10 = f32[512,256]{1,0:T(8,128)} fusion(bf16[512,2048]{1,0:T(8,128)(2,1)} %all-gather.13.cloned.1.call-done, bf16[2048,256]{1,0:T(8,128)(2,1)} %all-gather.11.cloned.1.call-done), kind=kOutput, calls=%fused_computation.17 | convolution fusion | flops 536870912 | bytes 3670016 | tf_op jit(solution)/shard_map/dot_general | solution.py:45
  108.8 24.1 %all-gather.15.cloned.1.call-done = bf16[2048,256]{1,0:T(8,128)(2,1)} async-done(((bf16[512,256]{1,0:T(8,128)(2,1)}), bf16[2048,256]{1,0:T(8,128)(2,1)}) %all-gather.15.cloned.1.call-update) | async-done | bytes 1048592 | tf_op jit(solution)/shard_map/all_gather | solution.py:44
  132.8 0.0 copy-done.1
  132.8 2.8 %fusion.4 = bf16[512,256]{1,0:T(8,128)(2,1)} fusion(f32[512,256]{1,0:T(8,128)} %fusion.10, bf16[512,2048]{1,0:T(8,128)(2,1)S(1)} %copy-done.1, bf16[2048,256]{1,0:T(8,128)(2,1)} %all-gather.15.cloned.1.call-done, f32[512,256]{1,0:T(8,128)S(1)} %get-tuple-element.6, f32[64,8,2,128]{3,2,1,0:T(2,128)S(1)} %bitcast.25), kind=kOutput, calls=%fused_computation.8 | convolution fusion | flops 537526272 | bytes 4980736 | tf_op jit(solution)/shard_map/dot_general | solution.py:50
  135.6 0.0 all-gather.19.cloned.1.call-update
  135.6 0.0 all-gather.17.cloned.1.call-start
  135.7 0.5 all-gather.17.cloned.1.call-update
  136.2 0.0 all-gather.21.cloned.1.call-start
  136.2 26.1 %all-gather.19.cloned.1.call-done = bf16[2048,256]{1,0:T(8,128)(2,1)} async-done(((bf16[512,256]{1,0:T(8,128)(2,1)}), bf16[2048,256]{1,0:T(8,128)(2,1)}) %all-gather.19.cloned.1.call-update) | async-done | bytes 1048592 | tf_op jit(solution)/shard_map/all_gather | solution.py:36
  162.4 32.3 %all-gather.17.cloned.1.call-done = bf16[512,2048]{1,0:T(8,128)(2,1)} async-done(((bf16[512,256]{1,0:T(8,128)(2,1)}), bf16[512,2048]{1,0:T(8,128)(2,1)}) %all-gather.17.cloned.1.call-update) | async-done | bytes 2097168 | tf_op jit(solution)/shard_map/all_gather | solution.py:38
  194.7 3.3 %fusion.9 = (bf16[512,256]{1,0:T(8,128)(2,1)}, f32[512,256]{1,0:T(8,128)S(1)}) fusion(f32[64,8,2,128]{3,2,1,0:T(2,128)S(1)} %bitcast.26, bf16[512,2048]{1,0:T(8,128)(2,1)} %all-gather.17.cloned.1.call-done, bf16[2048,256]{1,0:T(8,128)(2,1)} %all-gather.19.cloned.1.call-done), kind=kOutput, calls=%fused_computation.16 | convolution fusion | flops 537133056 | bytes 4456448 | tf_op jit(solution)/shard_map/dot_general | solution.py:37
  198.0 0.0 all-gather.21.cloned.1.call-update
  198.0 0.0 copy-start
  198.0 0.0 all-gather.23.cloned.1.call-start
  198.1 0.7 all-gather.23.cloned.1.call-update
  198.8 29.3 %all-gather.21.cloned.1.call-done = bf16[512,2048]{1,0:T(8,128)(2,1)} async-done(((bf16[512,256]{1,0:T(8,128)(2,1)}), bf16[512,2048]{1,0:T(8,128)(2,1)}) %all-gather.21.cloned.1.call-update) | async-done | bytes 2097168 | tf_op jit(solution)/shard_map/all_gather | solution.py:46
  228.1 3.4 %fusion.11 = f32[512,256]{1,0:T(8,128)} fusion(bf16[512,2048]{1,0:T(8,128)(2,1)} %all-gather.21.cloned.1.call-done, bf16[2048,256]{1,0:T(8,128)(2,1)} %all-gather.19.cloned.1.call-done), kind=kOutput, calls=%fused_computation.18 | convolution fusion | flops 536870912 | bytes 3670016 | tf_op jit(solution)/shard_map/dot_general | solution.py:45
  231.4 24.2 %all-gather.23.cloned.1.call-done = bf16[2048,256]{1,0:T(8,128)(2,1)} async-done(((bf16[512,256]{1,0:T(8,128)(2,1)}), bf16[2048,256]{1,0:T(8,128)(2,1)}) %all-gather.23.cloned.1.call-update) | async-done | bytes 1048592 | tf_op jit(solution)/shard_map/all_gather | solution.py:44
  255.6 0.0 copy-done
  255.6 2.9 %fusion.3 = f32[512,256]{1,0:T(8,128)} fusion(f32[512,256]{1,0:T(8,128)} %fusion.11, bf16[512,2048]{1,0:T(8,128)(2,1)S(1)} %copy-done, bf16[2048,256]{1,0:T(8,128)(2,1)} %all-gather.23.cloned.1.call-done, f32[512,256]{1,0:T(8,128)S(1)} %get-tuple-element.8, f32[64,8,2,128]{3,2,1,0:T(2,128)S(1)} %bitcast.27), kind=kOutput, calls=%fused_computation.7 | convolution fusion | flops 537395200 | bytes 5242880 | tf_op jit(solution)/shard_map/dot_general | solution.py:50
Async XLA Ops:
  6.5 33.0 %all-gather.11.cloned.1.call-start = ((), (), s32[]{:S(2)}) async-start(), calls=%async_computation.1 | async-start | bytes 1310720 | tf_op jit(solution)/shard_map/all_gather | solution.py:36
  10.1 61.9 %all-gather.9.cloned.1.call-start = ((), (), s32[]{:S(2)}) async-start(), calls=%async_computation | async-start | bytes 2359296 | tf_op jit(solution)/shard_map/all_gather | solution.py:38
  10.9 94.5 %all-gather.13.cloned.1.call-start = ((), (), s32[]{:S(2)}) async-start(), calls=%async_computation.2 | async-start | bytes 2359296 | tf_op jit(solution)/shard_map/all_gather | solution.py:46
  75.3 57.5 %copy-start.1 = (bf16[512,2048]{1,0:T(8,128)(2,1)S(1)}, bf16[512,2048]{1,0:T(8,128)(2,1)}, u32[]{:S(2)}) copy-start(bf16[512,2048]{1,0:T(8,128)(2,1)} %all-gather.9.cloned.1.call-done) | copy-start | bytes 6291460
  75.3 57.5 %all-gather.15.cloned.1.call-start = ((), (), s32[]{:S(2)}) async-start(), calls=%async_computation.3 | async-start | bytes 1310720 | tf_op jit(solution)/shard_map/all_gather | solution.py:44
  75.9 86.5 %all-gather.19.cloned.1.call-start = ((), (), s32[]{:S(2)}) async-start(), calls=%async_computation.5 | async-start | bytes 1310720 | tf_op jit(solution)/shard_map/all_gather | solution.py:36
  135.6 59.1 %all-gather.17.cloned.1.call-start = ((), (), s32[]{:S(2)}) async-start(), calls=%async_computation.4 | async-start | bytes 2359296 | tf_op jit(solution)/shard_map/all_gather | solution.py:38
  136.2 91.9 %all-gather.21.cloned.1.call-start = ((), (), s32[]{:S(2)}) async-start(), calls=%async_computation.6 | async-start | bytes 2359296 | tf_op jit(solution)/shard_map/all_gather | solution.py:46
  198.0 57.6 %copy-start = (bf16[512,2048]{1,0:T(8,128)(2,1)S(1)}, bf16[512,2048]{1,0:T(8,128)(2,1)}, u32[]{:S(2)}) copy-start(bf16[512,2048]{1,0:T(8,128)(2,1)} %all-gather.17.cloned.1.call-done) | copy-start | bytes 6291460
  198.0 57.6 %all-gather.23.cloned.1.call-start = ((), (), s32[]{:S(2)}) async-start(), calls=%async_computation.7 | async-start | bytes 1310720 | tf_op jit(solution)/shard_map/all_gather | solution.py:44
Sparse Core Ops, SparseCore 0:
  10.2 29.3 all-gather.10
  41.2 30.8 all-gather.8
  75.5 29.8 all-gather.12
  107.1 25.6 all-gather.14
  135.7 26.6 all-gather.18
  163.8 30.8 all-gather.16
  198.1 29.8 all-gather.20
  229.9 25.6 all-gather.22
where the time goes:
time: 266 us; the launch traced here: 265 us
  waiting for transfers between devices  229 us (86%)
  matrix products  18.9 us (7%)
  between operations  13.5 us (5%)
    all_gather x2, waiting for transfers between devices, on_device(): lax.all_gather(xb, 'col', axis=1, tiled=True)  64.8 us
    all_gather x2, waiting for transfers between devices, on_device(): lax.all_gather(qb, 'col', axis=1, tiled=True)  58.7 us
    all_gather x2, waiting for transfers between devices, on_device(): x_panel = lax.all_gather(xb, 'row', axis=0, tiled=True)  54.8 us
    all_gather x2, waiting for transfers between devices, on_device(): q_panel = lax.all_gather(qb, 'row', axis=0, tiled=True)  48.3 us
    dot_general x2, matrix products, on_device(): jnp.dot(lax.all_gather(qb, 'col', axis=1, tiled=True), x_panel, preferred...  6.72 us
    dot_general x2, matrix products, on_device(): jnp.dot(lax.all_gather(xb, 'col', axis=1, tiled=True), x_panel, preferred...  6.54 us
    dot_general x2, matrix products, on_device(): jnp.dot(lax.all_gather(xb, 'col', axis=1, tiled=True), q_panel, preferred...  5.63 us
  transfers between devices with their start and end apart: 8, of which 8 were waited for; matrix products, arithmetic and copies ran while one was open for 3% of the time, Pallas kernels for 0%

commit v1 on v0

--- a/solution.py
+++ b/solution.py
@@ -41,7 +41,25 @@
         )
         square = apply_mask(square, blocks)
         qb = square.astype(jnp.bfloat16)
-        q_panel = lax.all_gather(qb, "row", axis=0, tiled=True)
+        out_arr = lax.axis_size("row")
+        local_now = lax.axis_index("row")
+        m_next, y1, kept_arr = (out_arr, local_now, qb.shape[0])
+        column = [(t, (t + 1) % m_next) for t in range(m_next)]
+        views = [(t, (t - 1) % m_next) for t in range(m_next)]
+        q_panel = jnp.zeros((*qb.shape[:0], m_next * kept_arr, *qb.shape[1:]), qb.dtype)
+        q_panel = lax.dynamic_update_slice_in_dim(q_panel, qb, y1 * kept_arr, axis=0)
+        reached = inter = qb
+        k_now = m_next // 2
+        for dd in range(1, k_now + 1):
+            reached = lax.ppermute(reached, "row", column)
+            q_panel = lax.dynamic_update_slice_in_dim(
+                q_panel, reached, (y1 - dd) % m_next * kept_arr, axis=0
+            )
+            if dd < m_next - k_now:
+                inter = lax.ppermute(inter, "row", views)
+                q_panel = lax.dynamic_update_slice_in_dim(
+                    q_panel, inter, (y1 + dd) % m_next * kept_arr, axis=0
+                )
         total = jnp.dot(
             lax.all_gather(qb, "col", axis=1, tiled=True),
             x_panel,

time: 266 us -> 218 us (0.82)
  waiting for transfers between devices: 229 us -> 168 us
  local copies, waits for them, and re-layouts: 0.98 us -> 8.32 us
  starting transfers between devices: 0.28 us -> 6.76 us
    all_gather x2 -> x0, waiting for transfers between devices: 48.3 us -> none  [on_device(): q_panel = lax.all_gather(qb, 'row', axis=0, tiled=True)]
    all_gather x2, waiting for transfers between devices: 58.7 us -> 15.9 us  [on_device(): lax.all_gather(qb, 'col', axis=1, tiled=True)]
    ppermute x0 -> x6, waiting for transfers between devices: none -> 32.4 us  [the longest x4 23.7 us: on_device(): reached = lax.ppermute(reached, 'row', column)]
    ppermute x0 -> x6, starting transfers between devices: none -> 6.56 us  [the longest x2 3.45 us: on_device(): inter = lax.ppermute(inter, 'row', views)]
    dynamic_update_slice x0 -> x6, local copies, waits for them, and re-layouts: none -> 5.25 us  [the longest x4 3.8 us: on_device(): lax.dynamic_update_slice_in_dim(q_panel, reached, (y1 - dd) % m_next * ke...]
  transfers between devices with their start and end apart: 8 -> 12, of which waited for: 8 -> 12; matrix products, arithmetic and copies ran while one was open for 3% -> 2% of each run, Pallas kernels for 0% -> 0%
where the time goes in v1:
time: 218 us; the launch traced here: 217 us
  waiting for transfers between devices  168 us (77%)
  matrix products  17.2 us (8%)
  between operations  13.5 us (6%)
  local copies, waits for them, and re-layouts  8.32 us (4%)
  starting transfers between devices  6.76 us (3%)
  other arithmetic  2.56 us (1%)
    all_gather x2, waiting for transfers between devices, on_device(): lax.all_gather(xb, 'col', axis=1, tiled=True)  64.8 us
    all_gather x2, waiting for transfers between devices, on_device(): x_panel = lax.all_gather(xb, 'row', axis=0, tiled=True)  53.9 us
    ppermute x4, waiting for transfers between devices, on_device(): reached = lax.ppermute(reached, 'row', column)  23.7 us
    all_gather x2, waiting for transfers between devices, on_device(): lax.all_gather(qb, 'col', axis=1, tiled=True)  15.9 us
    ppermute x2, waiting for transfers between devices, on_device(): inter = lax.ppermute(inter, 'row', views)  8.66 us
    dot_general x2, matrix products, on_device(): jnp.dot(lax.all_gather(xb, 'col', axis=1, tiled=True), x_panel, preferred...  6.73 us
    dot_general x2, matrix products, on_device(): jnp.dot(lax.all_gather(xb, 'col', axis=1, tiled=True), q_panel, preferred...  5.38 us
    dot_general x2, matrix products, on_device(): jnp.dot(lax.all_gather(qb, 'col', axis=1, tiled=True), x_panel, preferred...  5.13 us
  transfers between devices with their start and end apart: 12, of which 12 were waited for; matrix products, arithmetic and copies ran while one was open for 2% of the time, Pallas kernels for 0%

profile of v1, /device:TPU:0, one launch (start us, length us, event | category | flops | bytes accessed | tf_op | source)
XLA Modules:
  0.0 216.6 jit_solution(2652369269332553832)
XLA Ops:
  6.5 0.0 all-gather.9.cloned.1.call-start
  6.5 0.8 copy.3
  7.3 0.8 fusion.7
  8.1 0.2 mul.69
  8.3 1.8 fusion.5
  10.1 0.0 all-gather.9.cloned.1.call-update
  10.1 0.0 all-gather.7.cloned.1.call-start
  10.2 0.7 all-gather.7.cloned.1.call-update
  10.9 0.0 all-gather.11.cloned.1.call-start
  10.9 28.7 %all-gather.9.cloned.1.call-done = bf16[2048,256]{1,0:T(8,128)(2,1)} async-done(((bf16[512,256]{1,0:T(8,128)(2,1)}), bf16[2048,256]{1,0:T(8,128)(2,1)}) %all-gather.9.cloned.1.call-update) | async-done | bytes 1048592 | tf_op jit(solution)/shard_map/all_gather | solution.py:36
  39.6 32.5 %all-gather.7.cloned.1.call-done = bf16[512,2048]{1,0:T(8,128)(2,1)} async-done(((bf16[512,256]{1,0:T(8,128)(2,1)}), bf16[512,2048]{1,0:T(8,128)(2,1)}) %all-gather.7.cloned.1.call-update) | async-done | bytes 2097168 | tf_op jit(solution)/shard_map/all_gather | solution.py:38
  72.0 1.0 broadcast.16.clone
  73.1 3.4 %constant_dynamic-update-slice_fusion.7 = (bf16[2048,256]{1,0:T(8,128)(2,1)}, bf16[512,256]{1,0:T(8,128)(2,1)}, f32[512,256]{1,0:T(8,128)S(1)}) fusion(bf16[2048,256]{1,0:T(8,128)(2,1)} %broadcast.16.clone, s32[]{:T(128)S(6)} %select_n.45, f32[64,8,2,128]{3,2,1,0:T(2,128)S(1)} %bitcast.24, bf16[512,2048]{1,0:T(8,128)(2,1)} %all-gather.7.cloned.1.call-done, ...), kind=kOutput, calls=%fused_computation.22 | convolution fusion | flops 537133056 | bytes 4718596 | tf_op jit(solution)/shard_map/dot_general | solution.py:37
  76.4 0.0 all-gather.11.cloned.1.call-update
  76.5 0.0 all-gather.15.cloned.1.call-start
  76.5 1.3 collective-permute-start
  77.8 1.7 collective-permute-start.1
  79.5 7.3 %collective-permute-done = bf16[512,256]{1,0:T(8,128)(2,1)S(1)} collective-permute-done((bf16[512,256]{1,0:T(8,128)(2,1)}, bf16[512,256]{1,0:T(8,128)(2,1)S(1)}, u32[]{:S(2)}, u32[]{:S(2)}) %collective-permute-start) | collective-permute-done | bytes 262176 | tf_op jit(solution)/shard_map/ppermute | solution.py:54
  86.8 0.3 collective-permute-start.2
  87.1 0.7 constant_dynamic-update-slice_fusion.6
  87.8 4.3 %collective-permute-done.1 = bf16[512,256]{1,0:T(8,128)(2,1)S(1)} collective-permute-done((bf16[512,256]{1,0:T(8,128)(2,1)}, bf16[512,256]{1,0:T(8,128)(2,1)S(1)}, u32[]{:S(2)}, u32[]{:S(2)}) %collective-permute-start.1) | collective-permute-done | bytes 262176 | tf_op jit(solution)/shard_map/ppermute | solution.py:59
  92.2 0.7 constant_dynamic-update-slice_fusion.5
  92.9 4.6 %collective-permute-done.2 = bf16[512,256]{1,0:T(8,128)(2,1)} collective-permute-done((bf16[512,256]{1,0:T(8,128)(2,1)S(1)}, bf16[512,256]{1,0:T(8,128)(2,1)}, u32[]{:S(2)}, u32[]{:S(2)}) %collective-permute-start.2) | collective-permute-done | bytes 262176 | tf_op jit(solution)/shard_map/ppermute | solution.py:54
  97.5 1.7 constant_dynamic-update-slice_fusion.4
  99.1 7.4 %all-gather.11.cloned.1.call-done = bf16[512,2048]{1,0:T(8,128)(2,1)} async-done(((bf16[512,256]{1,0:T(8,128)(2,1)}), bf16[512,2048]{1,0:T(8,128)(2,1)}) %all-gather.11.cloned.1.call-update) | async-done | bytes 2097168 | tf_op jit(solution)/shard_map/all_gather | solution.py:64
  106.5 2.6 %fusion.8 = f32[512,256]{1,0:T(8,128)S(1)} fusion(bf16[512,2048]{1,0:T(8,128)(2,1)} %all-gather.11.cloned.1.call-done, bf16[2048,256]{1,0:T(8,128)(2,1)} %all-gather.9.cloned.1.call-done), kind=kOutput, calls=%fused_computation.23 | convolution fusion | flops 536870912 | bytes 3670016 | tf_op jit(solution)/shard_map/dot_general | solution.py:63
  109.1 2.6 %fusion.4 = bf16[512,256]{1,0:T(8,128)(2,1)} fusion(f32[512,256]{1,0:T(8,128)S(1)} %fusion.8, bf16[512,2048]{1,0:T(8,128)(2,1)S(1)} %copy-done.1, bf16[2048,256]{1,0:T(8,128)(2,1)} %constant_dynamic-update-slice_fusion.4, f32[512,256]{1,0:T(8,128)S(1)} %get-tuple-element.9, f32[64,8,2,128]{3,2,1,0:T(2,128)S(1)} %bitcast.25), kind=kOutput, calls=%fused_computation.8 | convolution fusion | flops 537526272 | bytes 4980736 | tf_op jit(solution)/shard_map/dot_general | solution.py:68
  111.8 0.0 all-gather.15.cloned.1.call-update
  111.8 0.0 all-gather.13.cloned.1.call-start
  111.8 0.5 all-gather.13.cloned.1.call-update
  112.4 0.0 all-gather.17.cloned.1.call-start
  112.4 25.2 %all-gather.15.cloned.1.call-done = bf16[2048,256]{1,0:T(8,128)(2,1)} async-done(((bf16[512,256]{1,0:T(8,128)(2,1)}), bf16[2048,256]{1,0:T(8,128)(2,1)}) %all-gather.15.cloned.1.call-update) | async-done | bytes 1048592 | tf_op jit(solution)/shard_map/all_gather | solution.py:36
  137.6 32.3 %all-gather.13.cloned.1.call-done = bf16[512,2048]{1,0:T(8,128)(2,1)} async-done(((bf16[512,256]{1,0:T(8,128)(2,1)}), bf16[512,2048]{1,0:T(8,128)(2,1)}) %all-gather.13.cloned.1.call-update) | async-done | bytes 2097168 | tf_op jit(solution)/shard_map/all_gather | solution.py:38
  169.9 1.0 broadcast.16
  171.0 3.4 %constant_dynamic-update-slice_fusion.3 = (bf16[2048,256]{1,0:T(8,128)(2,1)}, bf16[512,256]{1,0:T(8,128)(2,1)}, f32[512,256]{1,0:T(8,128)S(1)}) fusion(bf16[2048,256]{1,0:T(8,128)(2,1)} %broadcast.16, s32[]{:T(128)S(6)} %select_n.45, f32[64,8,2,128]{3,2,1,0:T(2,128)S(1)} %bitcast.26, bf16[512,2048]{1,0:T(8,128)(2,1)} %all-gather.13.cloned.1.call-done, ...), kind=kOutput, calls=%fused_computation.18 | convolution fusion | flops 537133056 | bytes 4718596 | tf_op jit(solution)/shard_map/dot_general | solution.py:37
  174.4 0.0 all-gather.17.cloned.1.call-update
  174.4 1.3 collective-permute-start.3
  175.6 1.7 collective-permute-start.4
  177.4 7.3 %collective-permute-done.3 = bf16[512,256]{1,0:T(8,128)(2,1)S(1)} collective-permute-done((bf16[512,256]{1,0:T(8,128)(2,1)}, bf16[512,256]{1,0:T(8,128)(2,1)S(1)}, u32[]{:S(2)}, u32[]{:S(2)}) %collective-permute-start.3) | collective-permute-done | bytes 262176 | tf_op jit(solution)/shard_map/ppermute | solution.py:54
  184.7 0.3 collective-permute-start.5
  185.0 0.7 constant_dynamic-update-slice_fusion.2
  185.7 4.3 %collective-permute-done.4 = bf16[512,256]{1,0:T(8,128)(2,1)S(1)} collective-permute-done((bf16[512,256]{1,0:T(8,128)(2,1)}, bf16[512,256]{1,0:T(8,128)(2,1)S(1)}, u32[]{:S(2)}, u32[]{:S(2)}) %collective-permute-start.4) | collective-permute-done | bytes 262176 | tf_op jit(solution)/shard_map/ppermute | solution.py:59
  190.0 0.7 constant_dynamic-update-slice_fusion.1
  190.8 4.5 %collective-permute-done.5 = bf16[512,256]{1,0:T(8,128)(2,1)S(1)} collective-permute-done((bf16[512,256]{1,0:T(8,128)(2,1)S(1)}, bf16[512,256]{1,0:T(8,128)(2,1)S(1)}, u32[]{:S(2)}, u32[]{:S(2)}) %collective-permute-start.5) | collective-permute-done | bytes 262176 | tf_op jit(solution)/shard_map/ppermute | solution.py:54
  195.2 0.7 constant_dynamic-update-slice_fusion
  195.9 8.5 %all-gather.17.cloned.1.call-done = bf16[512,2048]{1,0:T(8,128)(2,1)} async-done(((bf16[512,256]{1,0:T(8,128)(2,1)}), bf16[512,2048]{1,0:T(8,128)(2,1)}) %all-gather.17.cloned.1.call-update) | async-done | bytes 2097168 | tf_op jit(solution)/shard_map/all_gather | solution.py:64
  204.4 2.6 %fusion.9 = f32[512,256]{1,0:T(8,128)S(1)} fusion(bf16[512,2048]{1,0:T(8,128)(2,1)} %all-gather.17.cloned.1.call-done, bf16[2048,256]{1,0:T(8,128)(2,1)} %all-gather.15.cloned.1.call-done), kind=kOutput, calls=%fused_computation.24 | convolution fusion | flops 536870912 | bytes 3670016 | tf_op jit(solution)/shard_map/dot_general | solution.py:63
  207.0 2.7 %fusion.3 = f32[512,256]{1,0:T(8,128)} fusion(f32[512,256]{1,0:T(8,128)S(1)} %fusion.9, bf16[512,2048]{1,0:T(8,128)(2,1)S(1)} %copy-done, bf16[2048,256]{1,0:T(8,128)(2,1)} %constant_dynamic-update-slice_fusion, f32[512,256]{1,0:T(8,128)S(1)} %get-tuple-element.10, f32[64,8,2,128]{3,2,1,0:T(2,128)S(1)} %bitcast.27), kind=kOutput, calls=%fused_computation.7 | convolution fusion | flops 537395200 | bytes 5242880 | tf_op jit(solution)/shard_map/dot_general | solution.py:68
  (4 shorter events, 0.0 us)
Async XLA Ops:
  6.5 33.0 %all-gather.9.cloned.1.call-start = ((), (), s32[]{:S(2)}) async-start(), calls=%async_computation.1 | async-start | bytes 1310720 | tf_op jit(solution)/shard_map/all_gather | solution.py:36
  10.1 61.9 %all-gather.7.cloned.1.call-start = ((), (), s32[]{:S(2)}) async-start(), calls=%async_computation | async-start | bytes 2359296 | tf_op jit(solution)/shard_map/all_gather | solution.py:38
  10.9 95.7 %all-gather.11.cloned.1.call-start = ((), (), s32[]{:S(2)}) async-start(), calls=%async_computation.2 | async-start | bytes 2359296 | tf_op jit(solution)/shard_map/all_gather | solution.py:64
  76.5 61.2 %all-gather.15.cloned.1.call-start = ((), (), s32[]{:S(2)}) async-start(), calls=%async_computation.4 | async-start | bytes 1310720 | tf_op jit(solution)/shard_map/all_gather | solution.py:36
  76.5 10.3 %collective-permute-start = (bf16[512,256]{1,0:T(8,128)(2,1)}, bf16[512,256]{1,0:T(8,128)(2,1)S(1)}, u32[]{:S(2)}, u32[]{:S(2)}) collective-permute-start(bf16[512,256]{1,0:T(8,128)(2,1)} %get-tuple-element.8), channel_id=1, source_target_pairs={{0,8},{8,16},{16,24},{24,0},{1,9},{9,17},{17,25},{25,1},{2,10},{10... | collective-permute-start | bytes 786440 | tf_op jit(solution)/shard_map/ppermute | solution.py:54
  77.8 14.4 %collective-permute-start.1 = (bf16[512,256]{1,0:T(8,128)(2,1)}, bf16[512,256]{1,0:T(8,128)(2,1)S(1)}, u32[]{:S(2)}, u32[]{:S(2)}) collective-permute-start(bf16[512,256]{1,0:T(8,128)(2,1)} %get-tuple-element.8), channel_id=1, source_target_pairs={{0,24},{8,0},{16,8},{24,16},{1,25},{9,1},{17,9},{25,17},{2,26},{10... | collective-permute-start | bytes 786440 | tf_op jit(solution)/shard_map/ppermute | solution.py:59
  86.8 10.7 %collective-permute-start.2 = (bf16[512,256]{1,0:T(8,128)(2,1)S(1)}, bf16[512,256]{1,0:T(8,128)(2,1)}, u32[]{:S(2)}, u32[]{:S(2)}) collective-permute-start(bf16[512,256]{1,0:T(8,128)(2,1)S(1)} %collective-permute-done), channel_id=1, source_target_pairs={{0,8},{8,16},{16,24},{24,0},{1,9},{9,17},{17,25},{25,1},{2,10},{10... | collective-permute-start | bytes 786440 | tf_op jit(solution)/shard_map/ppermute | solution.py:54
  92.9 16.2 %copy-start.1 = (bf16[512,2048]{1,0:T(8,128)(2,1)S(1)}, bf16[512,2048]{1,0:T(8,128)(2,1)}, u32[]{:S(2)}) copy-start(bf16[512,2048]{1,0:T(8,128)(2,1)} %all-gather.7.cloned.1.call-done) | copy-start | bytes 6291460
  111.8 58.2 %all-gather.13.cloned.1.call-start = ((), (), s32[]{:S(2)}) async-start(), calls=%async_computation.3 | async-start | bytes 2359296 | tf_op jit(solution)/shard_map/all_gather | solution.py:38
  112.4 92.1 %all-gather.17.cloned.1.call-start = ((), (), s32[]{:S(2)}) async-start(), calls=%async_computation.5 | async-start | bytes 2359296 | tf_op jit(solution)/shard_map/all_gather | solution.py:64
  174.4 10.3 %collective-permute-start.3 = (bf16[512,256]{1,0:T(8,128)(2,1)}, bf16[512,256]{1,0:T(8,128)(2,1)S(1)}, u32[]{:S(2)}, u32[]{:S(2)}) collective-permute-start(bf16[512,256]{1,0:T(8,128)(2,1)} %get-tuple-element.6), channel_id=1, source_target_pairs={{0,8},{8,16},{16,24},{24,0},{1,9},{9,17},{17,25},{25,1},{2,10},{10... | collective-permute-start | bytes 786440 | tf_op jit(solution)/shard_map/ppermute | solution.py:54
  175.6 14.4 %collective-permute-start.4 = (bf16[512,256]{1,0:T(8,128)(2,1)}, bf16[512,256]{1,0:T(8,128)(2,1)S(1)}, u32[]{:S(2)}, u32[]{:S(2)}) collective-permute-start(bf16[512,256]{1,0:T(8,128)(2,1)} %get-tuple-element.6), channel_id=1, source_target_pairs={{0,24},{8,0},{16,8},{24,16},{1,25},{9,1},{17,9},{25,17},{2,26},{10... | collective-permute-start | bytes 786440 | tf_op jit(solution)/shard_map/ppermute | solution.py:59
  184.7 10.6 %collective-permute-start.5 = (bf16[512,256]{1,0:T(8,128)(2,1)S(1)}, bf16[512,256]{1,0:T(8,128)(2,1)S(1)}, u32[]{:S(2)}, u32[]{:S(2)}) collective-permute-start(bf16[512,256]{1,0:T(8,128)(2,1)S(1)} %collective-permute-done.3), channel_id=1, source_target_pairs={{0,8},{8,16},{16,24},{24,0},{1,9},{9,17},{17,25},{25,1},{2,10},{10... | collective-permute-start | bytes 786440 | tf_op jit(solution)/shard_map/ppermute | solution.py:54
  190.7 16.3 %copy-start = (bf16[512,2048]{1,0:T(8,128)(2,1)S(1)}, bf16[512,2048]{1,0:T(8,128)(2,1)}, u32[]{:S(2)}) copy-start(bf16[512,2048]{1,0:T(8,128)(2,1)} %all-gather.13.cloned.1.call-done) | copy-start | bytes 6291460
Sparse Core Ops, SparseCore 0:
  10.2 29.3 all-gather.8
  41.2 30.8 all-gather.6
  76.6 29.8 all-gather.10
  111.9 25.6 all-gather.14
  139.1 30.8 all-gather.12
  174.5 29.8 all-gather.16
